TPU v7x, 512 devices: a whole 4x4x16 slice. The times are simulated.
512 devices in a mesh: row: 32 (over z, core), col: 16 (over x, y).
Axes of the slice: x: 4, y: 4, z: 16, core: 2. Of those that a mesh axis runs over, the one named last changes fastest.
Arguments:
- centroids: float32 [3, 16384], P(None, ('row', 'col')), may hold values from -4 to 4
- strengths: float32 [32, 16384], P(None, ('row', 'col')), may hold values from -6 to 6
- self_inv: float32 [32, 16384], P(None, ('row', 'col')), may hold values from -6 to 6
- wavenumbers: float32 [16], replicated, may hold values from 0.3 to 2
- field_pos: float32 [3, 8192], P(None, 'row'), may hold values from -4 to 4
- targets: float32 [32, 8192], P(None, 'row'), may hold values from -6 to 6
- lists: int32 [8192, 64], P('row'), may hold values from 0 to 16383
- connect: int32 [4, 16384], P(None, 'row'), may hold values from 0 to 16383, as said below
Outputs:
- adjoint: float32 [32, 16384], P(None, ('row', 'col'))
- vertex_sens: float32 [3, 16384], P(None, ('row', 'col'))
- objective: float32 [], replicated
Inputs may be any that keep to these rules, and one draw needn't show every extreme that they name: `connect`: the four vertices of panel i lie in the block of 512 vertices that starts at i - i % 512; the first of them is i itself.
All inputs are finite; a program needn't handle non-finite values.
Results may differ from a plain program's by a relative error of at most 0.0003.
Values sent between devices are 32-bit elements; how exact they have to be, the bound alone decides.
No kernel may reach another device: no remote copies, remote signals or barrier semaphores. Data moves between devices by JAX's collectives and lax.ppermute only.
A program may use at most 64 MiB of HBM per device.

v0:
```python
import math
import jax
import jax.numpy as jnp
from jax import lax
from jax.sharding import PartitionSpec as P

SOFT = 1.0


def pair_block(target_pos, target_str, target_mu, source_pos, source_str, source_mu, wavenumbers):
    freqs = wavenumbers.shape[0]
    offset = target_pos[:, None, :] - source_pos[:, :, None]
    squared = jnp.sum(offset * offset, axis=0) + SOFT
    inverse = lax.rsqrt(squared)
    distance = squared * inverse
    inverse_sq = inverse * inverse
    phase = wavenumbers[:, None, None] * distance[None]
    cosine = jnp.cos(phase)
    sine = jnp.sin(phase)
    deriv_real = -(cosine + phase * sine) * inverse_sq
    deriv_imag = (phase * cosine - sine) * inverse_sq
    tgt_real = target_str[:freqs, None, :]
    tgt_imag = target_str[freqs:, None, :]
    tmu_real = target_mu[:freqs, None, :]
    tmu_imag = target_mu[freqs:, None, :]
    src_real = source_str[:freqs, :, None]
    src_imag = source_str[freqs:, :, None]
    smu_real = source_mu[:freqs, :, None]
    smu_imag = source_mu[freqs:, :, None]
    prod_real = (
        tmu_real * src_real - tmu_imag * src_imag + smu_real * tgt_real - smu_imag * tgt_imag
    )
    prod_imag = (
        tmu_real * src_imag + tmu_imag * src_real + smu_real * tgt_imag + smu_imag * tgt_real
    )
    weight = jnp.sum(prod_real * deriv_real - prod_imag * deriv_imag, axis=0) * inverse
    return jnp.sum(weight[None] * offset, axis=1)


def pair_sweep(
    total, target_pos, target_str, target_mu, source_pos, source_str, source_mu, wavenumbers
):
    width = source_pos.shape[1]
    step = math.gcd(width, 128)

    def visit_block(carry, block_index):
        begin = block_index * step
        spos = lax.dynamic_slice_in_dim(source_pos, begin, step, 1)
        sstr = lax.dynamic_slice_in_dim(source_str, begin, step, 1)
        smu = lax.dynamic_slice_in_dim(source_mu, begin, step, 1)
        return (
            carry + pair_block(target_pos, target_str, target_mu, spos, sstr, smu, wavenumbers),
            None,
        )

    result, _ = lax.scan(visit_block, total, jnp.arange(width // step, dtype=jnp.int32))
    return result


def complex_times(left, right, freqs):
    left_real, left_imag = (left[:freqs], left[freqs:])
    right_real, right_imag = (right[:freqs], right[freqs:])
    return jnp.concatenate(
        [
            left_real * right_real - left_imag * right_imag,
            left_real * right_imag + left_imag * right_real,
        ],
        axis=0,
    )


def on_device(centroids, strengths, self_inv, wavenumbers, field_pos, targets, lists, connect):
    owned_count = centroids.shape[1]
    row_count = lax.axis_size("row")
    col_count = lax.axis_size("col")
    row_index = lax.axis_index("row")
    col_index = lax.axis_index("col")
    freqs = wavenumbers.shape[0]
    listed = lists.shape[1]
    panel_total = owned_count * row_count * col_count
    field_total = field_pos.shape[1] * row_count
    pos_rows = centroids.shape[0]
    str_rows = strengths.shape[0]
    owned = jnp.concatenate([centroids, strengths, self_inv], axis=0)
    src_all = lax.all_gather(owned, "row", axis=1, tiled=True)
    src_pos = src_all[:pos_rows]
    src_str = src_all[pos_rows : pos_rows + str_rows]
    src_inv = src_all[pos_rows + str_rows :]
    source_count = src_all.shape[1]
    panel_ids = lists.reshape(-1)
    owner_block = panel_ids // owned_count
    mask = (owner_block % col_count == col_index).astype(jnp.float32)
    local_ids = owner_block // col_count * owned_count + panel_ids % owned_count
    near_all = jnp.take(src_all[: pos_rows + str_rows], local_ids, axis=1)
    near = near_all[:pos_rows]
    observer = jnp.repeat(field_pos, listed, axis=1)
    offset = observer - near
    distance = jnp.sqrt(jnp.sum(offset * offset, axis=0) + SOFT)
    inverse = mask / distance
    phase = wavenumbers[:, None] * distance[None]
    cosine = jnp.cos(phase)
    sine = jnp.sin(phase)
    near_str = near_all[pos_rows:]
    str_real = near_str[:freqs]
    str_imag = near_str[freqs:]
    part_real = (cosine * str_real - sine * str_imag) * inverse
    part_imag = (cosine * str_imag + sine * str_real) * inverse
    eta_part = jnp.concatenate(
        [
            part_real.reshape(freqs, -1, listed).sum(axis=2),
            part_imag.reshape(freqs, -1, listed).sum(axis=2),
        ],
        axis=0,
    )
    eta = lax.psum(eta_part, "col")
    resid = eta - targets
    rep_real = jnp.repeat(resid[:freqs], listed, axis=1)
    rep_imag = jnp.repeat(resid[freqs:], listed, axis=1)
    term_real = (cosine * rep_real + sine * rep_imag) * inverse
    term_imag = (cosine * rep_imag - sine * rep_real) * inverse
    terms = jnp.concatenate([term_real, term_imag], axis=0)
    source_part = jnp.zeros((2 * freqs, source_count), jnp.float32).at[:, local_ids].add(terms)
    misfit_part = jnp.sum(resid * resid)
    misfit_row = jnp.where(
        lax.broadcasted_iota(jnp.int32, (1, source_count), 1) == 0, misfit_part, 0.0
    )
    packed = lax.psum(jnp.concatenate([source_part, misfit_row], axis=0), "row")
    objective = packed[2 * freqs, 0] / (freqs * field_total) + 1e-06
    source_all = packed[: 2 * freqs] / objective
    mu_all = complex_times(source_all, src_inv, freqs)
    mu_own = lax.dynamic_slice_in_dim(mu_all, row_index * owned_count, owned_count, 1)
    tgt_all = lax.all_gather(
        jnp.concatenate([centroids, strengths, mu_own], axis=0), "col", axis=1, tiled=True
    )
    tgt_pos = tgt_all[:pos_rows]
    tgt_str = tgt_all[pos_rows : pos_rows + str_rows]
    tgt_mu = tgt_all[pos_rows + str_rows :]
    block_width = tgt_pos.shape[1]
    empty = jnp.zeros((3, block_width), jnp.float32)
    accum = pair_sweep(empty, tgt_pos, tgt_str, tgt_mu, src_pos, src_str, mu_all, wavenumbers)
    panel_sens = accum * (1.0 / math.sqrt(panel_total * freqs))
    vertex_local = connect - row_index * block_width
    vertex_part = (
        jnp.zeros((3, block_width), jnp.float32)
        .at[:, vertex_local.reshape(-1)]
        .add(jnp.tile(0.25 * panel_sens, (1, connect.shape[0])))
    )
    vertex_own = lax.psum_scatter(vertex_part, "col", scatter_dimension=1, tiled=True)
    adjoint = mu_own
    return (adjoint, vertex_own, objective)


def solution(mesh):
    return jax.shard_map(
        on_device,
        mesh=mesh,
        in_specs=(
            P(None, ("row", "col")),
            P(None, ("row", "col")),
            P(None, ("row", "col")),
            P(),
            P(None, "row"),
            P(None, "row"),
            P("row", None),
            P(None, "row"),
        ),
        out_specs=(P(None, ("row", "col")), P(None, ("row", "col")), P()),
        check_vma=False,
    )
```

profile of v0, /device:TPU:2, one launch (start us, length us, event | category | flops | bytes accessed | tf_op | source)
XLA Modules:
  0.0 815.2 jit_solution(18227825335642472802)
XLA Ops:
  7.2 0.9 copy.140
  8.4 0.8 copy.142
  9.2 0.8 copy.143
  10.0 0.8 copy.144
  10.8 37.6 %all_gather.6 = f32[67,1024]{0,1:T(8,128)S(1)} all-gather(f32[67,32]{0,1:T(8,128)S(1)} %pad_maximum_fusion.3), channel_id=1, replica_groups=mesh['row'=32,'col'=16] {'row'}, dimensions={1}, use_global_device_ids=true | all-gather | bytes 283008 | tf_op jit(solution)/shard_map/all_gather | solution.py:85
  48.5 0.8 compare_select_fusion
  49.3 0.6 copy-done.3
  49.9 54.4 %gather_fusion = f32[16384,35]{1,0:T(8,128)} fusion(f32[35,1024]{0,1:T(8,128)S(1)} %bitcast.25, s32[16384]{0:T(1024)S(1)} %broadcast_clamp_fusion), kind=kCustom, calls=%fused_computation | custom fusion | bytes 4653056 | tf_op jit(solution)/shard_map/jit(_take)/gather | solution.py:94
  104.4 5.3 copy.145
  109.6 0.7 compare_and_fusion
  110.4 0.8 broadcast_in_dim.27
  111.2 0.9 reshape.314
  112.1 1.0 select_bitcast_fusion
  113.1 0.2 fusion.29
  113.4 4.4 fusion.20
  117.8 4.6 copy.163
  122.4 5.0 bitcast_reduce_fusion.1
  127.6 4.6 copy.164
  132.2 5.1 bitcast_reduce_fusion
  137.3 68.6 %psum.14 = f32[32,256]{1,0:T(8,128)S(1)} all-reduce(f32[32,256]{1,0:T(8,128)S(1)} %pad_maximum_fusion.2), channel_id=1, replica_groups=mesh['row'=32,'col'=16] {'col'}, use_global_device_ids=true, to_apply=%region_3.4 | all-reduce | flops 8192 | bytes 65536 | tf_op jit(solution)/shard_map/psum | solution.py:115
  205.9 0.6 multiply_reduce_fusion
  206.5 0.6 broadcast_in_dim.30
  207.1 1.7 reshape.318
  208.8 0.6 broadcast_in_dim.31
  209.4 1.6 reshape.319
  211.0 6.8 fusion.24
  218.0 4.7 copy.150
  222.7 0.7 fusion.27
  223.4 87.7 %scatter_custom_fusion = f32[32,1024]{0,1:T(8,128)S(1)} fusion(s32[16384]{0:T(1024)} %bitcast.30, f32[16384,32]{1,0:T(8,128)} %copy.150, f32[]{:T(128)} %constant.96.clone.1), kind=kCustom, calls=%fused_computation.59 | custom fusion | flops 524288 | bytes 131584 | tf_op jit(solution)/shard_map/scatter-add | solution.py:122
  311.1 1.0 pad_maximum_fusion
  312.3 0.2 slice.121
  312.5 0.2 copy.157
  312.7 0.2 copy.160
  312.9 204.5 %all-reduce.2.cloned.1.call-done = f32[33,1024]{0,1:T(8,128)} async-done(((f32[33,1024]{0,1:T(8,128)}), f32[33,1024]{0,1:T(8,128)}) %all-reduce.2.cloned.1.call-update) | async-done | bytes 135184 | tf_op jit(solution)/shard_map/psum | solution.py:127
  517.3 1.3 slice.115
  519.3 1.1 slice_divide_fusion
  520.3 0.5 multiply_add_fusion
  521.0 0.2 copy.152
  521.4 23.7 %all_gather.7 = f32[67,512]{0,1:T(8,128)S(1)} all-gather(f32[67,32]{0,1:T(8,128)S(1)} %pad_maximum_fusion.5), channel_id=1, replica_groups=mesh['row'=32,'col'=16] {'col'}, dimensions={1}, use_global_device_ids=true | all-gather | bytes 145792 | tf_op jit(solution)/shard_map/all_gather | solution.py:132
  545.1 0.2 fusion.45
  545.6 162.3 %while.11 = (s32[]{:T(128)}, f32[3,512]{1,0:T(4,128)S(1)}, f32[32,512]{1,0:T(8,128)S(1)}, s32[8]{0:T(128)S(1)}, f32[32,1024]{1,0:T(8,128)S(1)}, /*index=5*/f32[3...) while((s32[]{:T(128)}, f32[3,512]{1,0:T(4,128)S(1)}, ...), condition=%wide.region_11.12_spmd.clone, body=%wide.region_7.11_spmd.clone.sunk | while | flops 28640776 | bytes 3418409 | solution.py:56
  545.6 0.7 dynamic_slice.33
  547.3 18.4 %fusion.53 = f32[128,512]{1,0:T(8,128)S(1)} fusion(f32[128,512]{1,0:T(8,128)S(1)} %get-tuple-element.299, f32[128,512]{1,0:T(8,128)S(1)} %get-tuple-element.300, f32[16]{0:T(128)S(1)} %get-tuple-element.346, f32[16,512]{1,0:T(8,128)S(1)} %get-tuple-element.301, f32[16,128]{1,0:T(8,128)S(1)} %get-tuple-element.302, ...), kind=kLoop, calls=%fused_computation.12.clone.1 | loop fusion | flops 27197440 | bytes 950336 | tf_op jit(solution)/shard_map/while/body/eval_jaxpr/reduce_sum | solution.py:36
  565.9 0.7 dynamic_slice.33
  567.6 18.4 %fusion.53 = f32[128,512]{1,0:T(8,128)S(1)} fusion(f32[128,512]{1,0:T(8,128)S(1)} %get-tuple-element.299, f32[128,512]{1,0:T(8,128)S(1)} %get-tuple-element.300, f32[16]{0:T(128)S(1)} %get-tuple-element.346, f32[16,512]{1,0:T(8,128)S(1)} %get-tuple-element.301, f32[16,128]{1,0:T(8,128)S(1)} %get-tuple-element.302, ...), kind=kLoop, calls=%fused_computation.12.clone.1 | loop fusion | flops 27197440 | bytes 950336 | tf_op jit(solution)/shard_map/while/body/eval_jaxpr/reduce_sum | solution.py:36
  586.0 0.2 fusion.54
  586.2 0.7 dynamic_slice.33
  587.8 18.4 %fusion.53 = f32[128,512]{1,0:T(8,128)S(1)} fusion(f32[128,512]{1,0:T(8,128)S(1)} %get-tuple-element.299, f32[128,512]{1,0:T(8,128)S(1)} %get-tuple-element.300, f32[16]{0:T(128)S(1)} %get-tuple-element.346, f32[16,512]{1,0:T(8,128)S(1)} %get-tuple-element.301, f32[16,128]{1,0:T(8,128)S(1)} %get-tuple-element.302, ...), kind=kLoop, calls=%fused_computation.12.clone.1 | loop fusion | flops 27197440 | bytes 950336 | tf_op jit(solution)/shard_map/while/body/eval_jaxpr/reduce_sum | solution.py:36
  606.5 0.7 dynamic_slice.33
  608.1 18.4 %fusion.53 = f32[128,512]{1,0:T(8,128)S(1)} fusion(f32[128,512]{1,0:T(8,128)S(1)} %get-tuple-element.299, f32[128,512]{1,0:T(8,128)S(1)} %get-tuple-element.300, f32[16]{0:T(128)S(1)} %get-tuple-element.346, f32[16,512]{1,0:T(8,128)S(1)} %get-tuple-element.301, f32[16,128]{1,0:T(8,128)S(1)} %get-tuple-element.302, ...), kind=kLoop, calls=%fused_computation.12.clone.1 | loop fusion | flops 27197440 | bytes 950336 | tf_op jit(solution)/shard_map/while/body/eval_jaxpr/reduce_sum | solution.py:36
  626.6 0.2 fusion.54
  626.8 0.7 dynamic_slice.33
  628.4 18.4 %fusion.53 = f32[128,512]{1,0:T(8,128)S(1)} fusion(f32[128,512]{1,0:T(8,128)S(1)} %get-tuple-element.299, f32[128,512]{1,0:T(8,128)S(1)} %get-tuple-element.300, f32[16]{0:T(128)S(1)} %get-tuple-element.346, f32[16,512]{1,0:T(8,128)S(1)} %get-tuple-element.301, f32[16,128]{1,0:T(8,128)S(1)} %get-tuple-element.302, ...), kind=kLoop, calls=%fused_computation.12.clone.1 | loop fusion | flops 27197440 | bytes 950336 | tf_op jit(solution)/shard_map/while/body/eval_jaxpr/reduce_sum | solution.py:36
  647.1 0.7 dynamic_slice.33
  648.7 18.4 %fusion.53 = f32[128,512]{1,0:T(8,128)S(1)} fusion(f32[128,512]{1,0:T(8,128)S(1)} %get-tuple-element.299, f32[128,512]{1,0:T(8,128)S(1)} %get-tuple-element.300, f32[16]{0:T(128)S(1)} %get-tuple-element.346, f32[16,512]{1,0:T(8,128)S(1)} %get-tuple-element.301, f32[16,128]{1,0:T(8,128)S(1)} %get-tuple-element.302, ...), kind=kLoop, calls=%fused_computation.12.clone.1 | loop fusion | flops 27197440 | bytes 950336 | tf_op jit(solution)/shard_map/while/body/eval_jaxpr/reduce_sum | solution.py:36
  667.1 0.2 fusion.54
  667.3 0.7 dynamic_slice.33
  669.0 18.4 %fusion.53 = f32[128,512]{1,0:T(8,128)S(1)} fusion(f32[128,512]{1,0:T(8,128)S(1)} %get-tuple-element.299, f32[128,512]{1,0:T(8,128)S(1)} %get-tuple-element.300, f32[16]{0:T(128)S(1)} %get-tuple-element.346, f32[16,512]{1,0:T(8,128)S(1)} %get-tuple-element.301, f32[16,128]{1,0:T(8,128)S(1)} %get-tuple-element.302, ...), kind=kLoop, calls=%fused_computation.12.clone.1 | loop fusion | flops 27197440 | bytes 950336 | tf_op jit(solution)/shard_map/while/body/eval_jaxpr/reduce_sum | solution.py:36
  687.6 0.7 dynamic_slice.33
  689.3 18.4 %fusion.53 = f32[128,512]{1,0:T(8,128)S(1)} fusion(f32[128,512]{1,0:T(8,128)S(1)} %get-tuple-element.299, f32[128,512]{1,0:T(8,128)S(1)} %get-tuple-element.300, f32[16]{0:T(128)S(1)} %get-tuple-element.346, f32[16,512]{1,0:T(8,128)S(1)} %get-tuple-element.301, f32[16,128]{1,0:T(8,128)S(1)} %get-tuple-element.302, ...), kind=kLoop, calls=%fused_computation.12.clone.1 | loop fusion | flops 27197440 | bytes 950336 | tf_op jit(solution)/shard_map/while/body/eval_jaxpr/reduce_sum | solution.py:36
  707.7 0.2 fusion.54
  708.1 12.1 %scatter_custom_fusion.1 = f32[3,512]{0,1:T(8,128)} fusion(s32[2048]{0:T(1024)S(1)} %bitcast.32, f32[2048,3]{1,0:T(8,128)S(1)} %bitcast.28, f32[]{:T(128)} %constant.96.clone.1), kind=kCustom, calls=%fused_computation.74 | custom fusion | flops 6144 | bytes 6148 | tf_op jit(solution)/shard_map/scatter-add | solution.py:146
  720.3 85.6 %reduce-scatter.2.cloned.1.call-done = f32[3,32]{0,1:T(8,128)} async-done(((f32[3,512]{0,1:T(8,128)}), f32[3,32]{0,1:T(8,128)}) %reduce-scatter.2.cloned.1.call-update) | async-done | bytes 400 | tf_op jit(solution)/shard_map/reduce_scatter | solution.py:148
  805.9 1.4 copy.162
  (109 shorter events, 4.8 us)
Async XLA Ops:
  7.2 510.2 %all-reduce.2.cloned.1.call-start = ((), (), s32[]{:S(2)}) async-start(), calls=%async_computation.1 | async-start | bytes 1048576 | tf_op jit(solution)/shard_map/psum | solution.py:127
  8.4 101.3 %copy-start.1 = (s32[16384]{0:T(1024)}, s32[16384]{0:T(1024)S(1)}, u32[]{:S(2)}) copy-start(s32[16384]{0:T(1024)S(1)} %reshape.315) | copy-start | bytes 196612
  10.0 94.4 %copy-start.4 = (f32[32,32]{0,1:T(8,128)}, f32[32,32]{0,1:T(8,128)S(1)}, u32[]{:S(2)}) copy-start(f32[32,32]{0,1:T(8,128)S(1)} %copy.143) | copy-start | bytes 12292
  49.3 0.6 copy-start.3
  112.1 1.0 copy-start
  112.1 1.2 copy-start.2
  112.1 1.3 copy-start.9
  132.2 73.7 %copy-start.7 = (f32[32,256]{1,0:T(8,128)S(1)}, f32[32,256]{1,0:T(8,128)}, u32[]{:S(2)}) copy-start(f32[32,256]{1,0:T(8,128)} %param.15) | copy-start | bytes 98308
  218.0 94.2 %copy-start.8 = (s32[4,512]{1,0:T(4,128)S(1)}, s32[4,512]{1,0:T(4,128)}, u32[]{:S(2)}) copy-start(s32[4,512]{1,0:T(4,128)} %param.17) | copy-start | bytes 24580
  312.2 209.2 %copy-start.5 = (f32[32,32]{0,1:T(8,128)S(1)}, f32[32,32]{0,1:T(8,128)}, u32[]{:S(2)}) copy-start(f32[32,32]{0,1:T(8,128)} %copy-done.4) | copy-start | bytes 12292
  312.2 493.7 %reduce-scatter.2.cloned.1.call-start = ((), (), s32[]{:S(2)}) async-start(), calls=%async_computation.2 | async-start | bytes 278528 | tf_op jit(solution)/shard_map/reduce_scatter | solution.py:148
  521.3 24.4 %copy-start.6 = (f32[32,32]{1,0:T(8,128)}, f32[32,32]{1,0:T(8,128)S(1)}, u32[]{:S(2)}) copy-start(f32[32,32]{1,0:T(8,128)S(1)} %fusion.42) | copy-start | bytes 12292
Sparse Core Ops, SparseCore 0:
  312.3 205.0 all-reduce.1
  720.4 85.4 reduce-scatter.1
where the time goes:
time: 816 us; the launch traced here: 815 us
  waiting for transfers between devices  290 us (36%)
  other arithmetic  279 us (34%)
  blocking collectives  130 us (16%)
  local copies, waits for them, and re-layouts  94.1 us (12%)
  between operations  16.1 us (2%)
    psum x1, waiting for transfers between devices, on_device(): packed = lax.psum(jnp.concatenate([source_part, misfit_row], axis=0), 'row')  204 us
    reduce_sum x8, other arithmetic, pair_block(): jnp.sum(prod_real * deriv_real - prod_imag * deriv_imag, axis=0) * inverse  147 us
    scatter-add x1, other arithmetic, on_device(): jnp.zeros((2 * freqs, source_count), jnp.float32).at[:, local_ids]  87.7 us
    reduce_scatter x1, waiting for transfers between devices, on_device(): lax.psum_scatter(vertex_part, 'col', scatter_dimension=1, tiled=True)  85.6 us
    psum x1, blocking collectives, on_device(): eta = lax.psum(eta_part, 'col')  68.6 us
    gather x2, local copies, waits for them, and re-layouts, on_device(): near_all = jnp.take(src_all[:pos_rows + str_rows], local_ids, axis=1)  59.7 us
    all_gather x1, blocking collectives, on_device(): src_all = lax.all_gather(owned, 'row', axis=1, tiled=True)  37.6 us
    all_gather x1, blocking collectives, on_device(): lax.all_gather(jnp.concatenate([centroids, strengths, mu_own], axis=0), '...  23.7 us
  transfers between devices with their start and end apart: 2, of which 2 were waited for; matrix products, arithmetic and copies ran while one was open for 0% of the time, Pallas kernels for 0%

commit v1 on v0

--- a/solution.py
+++ b/solution.py
@@ -124,7 +124,9 @@
     misfit_row = jnp.where(
         lax.broadcasted_iota(jnp.int32, (1, source_count), 1) == 0, misfit_part, 0.0
     )
-    packed = lax.psum(jnp.concatenate([source_part, misfit_row], axis=0), "row")
+    packed = jnp.sum(
+        lax.all_gather(jnp.concatenate([source_part, misfit_row], axis=0), "row"), axis=0
+    )
     objective = packed[2 * freqs, 0] / (freqs * field_total) + 1e-06
     source_all = packed[: 2 * freqs] / objective
     mu_all = complex_times(source_all, src_inv, freqs)

time: 816 us -> 681 us (0.83)
  waiting for transfers between devices: 290 us -> 154 us
    psum x1 -> x0, waiting for transfers between devices: 204 us -> none  [on_device(): packed = lax.psum(jnp.concatenate([source_part, misfit_row], axis=0), 'row')]
    all_gather x0 -> x1, waiting for transfers between devices: none -> 72.2 us  [on_device(): lax.all_gather(jnp.concatenate([source_part, misfit_row], axis=0), 'row')]
where the time goes in v1:
time: 681 us; the launch traced here: 680 us
  other arithmetic  280 us (41%)
  waiting for transfers between devices  154 us (23%)
  blocking collectives  130 us (19%)
  local copies, waits for them, and re-layouts  93.8 us (14%)
  between operations  16.1 us (2%)
    reduce_sum x8, other arithmetic, pair_block(): jnp.sum(prod_real * deriv_real - prod_imag * deriv_imag, axis=0) * inverse  147 us
    scatter-add x1, other arithmetic, on_device(): jnp.zeros((2 * freqs, source_count), jnp.float32).at[:, local_ids]  87.7 us
    reduce_scatter x1, waiting for transfers between devices, on_device(): lax.psum_scatter(vertex_part, 'col', scatter_dimension=1, tiled=True)  82.1 us
    all_gather x1, waiting for transfers between devices, on_device(): lax.all_gather(jnp.concatenate([source_part, misfit_row], axis=0), 'row')  72.2 us
    psum x1, blocking collectives, on_device(): eta = lax.psum(eta_part, 'col')  68.6 us
    gather x2, local copies, waits for them, and re-layouts, on_device(): near_all = jnp.take(src_all[:pos_rows + str_rows], local_ids, axis=1)  59.7 us
    all_gather x1, blocking collectives, on_device(): src_all = lax.all_gather(owned, 'row', axis=1, tiled=True)  37.6 us
    all_gather x1, blocking collectives, on_device(): lax.all_gather(jnp.concatenate([centroids, strengths, mu_own], axis=0), '...  23.7 us
  transfers between devices with their start and end apart: 2, of which 2 were waited for; matrix products, arithmetic and copies ran while one was open for 0% of the time, Pallas kernels for 0%

profile of v1, /device:TPU:2, one launch (start us, length us, event | category | flops | bytes accessed | tf_op | source)
XLA Modules:
  0.0 680.5 jit_solution(17785406377580188875)
XLA Ops:
  7.2 0.9 copy.143
  8.4 0.8 copy.145
  9.2 0.8 copy.146
  10.0 0.8 copy.147
  10.8 37.6 %all_gather.12 = f32[67,1024]{0,1:T(8,128)S(1)} all-gather(f32[67,32]{0,1:T(8,128)S(1)} %pad_maximum_fusion.2), channel_id=1, replica_groups=mesh['row'=32,'col'=16] {'row'}, dimensions={1}, use_global_device_ids=true | all-gather | bytes 283008 | tf_op jit(solution)/shard_map/all_gather | solution.py:85
  48.5 0.8 compare_select_fusion
  49.3 0.6 copy-done.3
  49.9 54.4 %gather_fusion = f32[16384,35]{1,0:T(8,128)} fusion(f32[35,1024]{0,1:T(8,128)S(1)} %bitcast.27, s32[16384]{0:T(1024)S(1)} %broadcast_clamp_fusion), kind=kCustom, calls=%fused_computation | custom fusion | bytes 4653056 | tf_op jit(solution)/shard_map/jit(_take)/gather | solution.py:94
  104.4 5.3 copy.148
  109.6 0.7 compare_and_fusion
  110.4 0.8 broadcast_in_dim.27
  111.2 0.9 reshape.314
  112.1 1.0 select_bitcast_fusion
  113.1 0.2 fusion.28
  113.4 4.4 fusion.20
  117.8 4.6 copy.168
  122.4 5.0 bitcast_reduce_fusion.1
  127.6 4.6 copy.169
  132.2 5.1 bitcast_reduce_fusion
  137.3 68.6 %psum.7 = f32[32,256]{1,0:T(8,128)S(1)} all-reduce(f32[32,256]{1,0:T(8,128)S(1)} %pad_maximum_fusion.1), channel_id=1, replica_groups=mesh['row'=32,'col'=16] {'col'}, use_global_device_ids=true, to_apply=%region_3.4 | all-reduce | flops 8192 | bytes 65536 | tf_op jit(solution)/shard_map/psum | solution.py:115
  205.9 0.6 multiply_reduce_fusion
  206.5 0.6 broadcast_in_dim.30
  207.1 1.7 reshape.318
  208.8 0.6 broadcast_in_dim.31
  209.4 1.6 reshape.319
  211.0 6.8 %fusion.24 = (f32[16,16384]{1,0:T(8,128)S(1)}, f32[16,16384]{1,0:T(8,128)S(1)}) fusion(f32[16,16384]{1,0:T(8,128)} %reshape.319, f32[16,16384]{1,0:T(8,128)} %reshape.318, f32[16384]{0:T(1024)S(1)} %get-tuple-element.225, f32[16384]{0:T(1024)S(1)} %get-tuple-element.224, f32[16]{0:T(128)S(1)} %copy-done.9), kind=kLoop, calls=%fused_computation.46 | loop fusion | flops 2359296 | bytes 4325440 | tf_op jit(solution)/shard_map/mul | solution.py:119
  218.0 4.7 copy.153
  222.7 87.7 %scatter_custom_fusion = f32[32,1024]{0,1:T(8,128)S(1)} fusion(s32[16384]{0:T(1024)} %bitcast.32, f32[16384,32]{1,0:T(8,128)} %copy.153, f32[]{:T(128)} %constant.96.clone.1), kind=kCustom, calls=%fused_computation.56 | custom fusion | flops 524288 | bytes 131584 | tf_op jit(solution)/shard_map/scatter-add | solution.py:122
  310.4 0.2 copy.154
  310.6 0.7 compare_select_fusion.9
  311.3 0.7 maximum_bitcast_fusion.1
  312.0 0.2 slice.121
  312.2 0.2 copy.162
  312.4 0.2 copy.165
  312.6 72.2 %all-gather.4.cloned.1.call-done = f32[32,33,1024]{2,1,0:T(8,128)} async-done(((f32[1,33,1024]{2,1,0:T(8,128)}), f32[32,33,1024]{2,1,0:T(8,128)}) %all-gather.4.cloned.1.call-update) | async-done | bytes 4325392 | tf_op jit(solution)/shard_map/all_gather | solution.py:128
  384.8 2.8 reduce_sum.76
  387.7 0.5 slice.115
  388.2 0.2 copy.170
  389.1 0.5 multiply_add_fusion
  389.7 0.2 copy.157
  390.2 23.7 %all_gather.15 = f32[67,512]{0,1:T(8,128)S(1)} all-gather(f32[67,32]{0,1:T(8,128)S(1)} %pad_maximum_fusion.4), channel_id=1, replica_groups=mesh['row'=32,'col'=16] {'col'}, dimensions={1}, use_global_device_ids=true | all-gather | bytes 145792 | tf_op jit(solution)/shard_map/all_gather | solution.py:134
  413.8 0.2 fusion.44
  414.4 162.3 %while.11 = (s32[]{:T(128)}, f32[3,512]{1,0:T(4,128)S(1)}, f32[32,512]{1,0:T(8,128)S(1)}, s32[8]{0:T(128)S(1)}, f32[32,1024]{1,0:T(8,128)S(1)}, /*index=5*/f32[3...) while((s32[]{:T(128)}, f32[3,512]{1,0:T(4,128)S(1)}, ...), condition=%wide.region_11.12_spmd.clone, body=%wide.region_7.11_spmd.clone.sunk | while | flops 28640776 | bytes 3418409 | solution.py:56
  414.4 0.7 dynamic_slice.33
  416.0 18.4 %fusion.52 = f32[128,512]{1,0:T(8,128)S(1)} fusion(f32[128,512]{1,0:T(8,128)S(1)} %get-tuple-element.299, f32[128,512]{1,0:T(8,128)S(1)} %get-tuple-element.300, f32[16]{0:T(128)S(1)} %get-tuple-element.346, f32[16,512]{1,0:T(8,128)S(1)} %get-tuple-element.301, f32[16,128]{1,0:T(8,128)S(1)} %get-tuple-element.302, ...), kind=kLoop, calls=%fused_computation.12.clone.1 | loop fusion | flops 27197440 | bytes 950336 | tf_op jit(solution)/shard_map/while/body/eval_jaxpr/reduce_sum | solution.py:36
  434.5 0.2 fusion.53
  434.7 0.7 dynamic_slice.33
  436.3 18.4 %fusion.52 = f32[128,512]{1,0:T(8,128)S(1)} fusion(f32[128,512]{1,0:T(8,128)S(1)} %get-tuple-element.299, f32[128,512]{1,0:T(8,128)S(1)} %get-tuple-element.300, f32[16]{0:T(128)S(1)} %get-tuple-element.346, f32[16,512]{1,0:T(8,128)S(1)} %get-tuple-element.301, f32[16,128]{1,0:T(8,128)S(1)} %get-tuple-element.302, ...), kind=kLoop, calls=%fused_computation.12.clone.1 | loop fusion | flops 27197440 | bytes 950336 | tf_op jit(solution)/shard_map/while/body/eval_jaxpr/reduce_sum | solution.py:36
  454.8 0.2 fusion.53
  455.0 0.7 dynamic_slice.33
  456.6 18.4 %fusion.52 = f32[128,512]{1,0:T(8,128)S(1)} fusion(f32[128,512]{1,0:T(8,128)S(1)} %get-tuple-element.299, f32[128,512]{1,0:T(8,128)S(1)} %get-tuple-element.300, f32[16]{0:T(128)S(1)} %get-tuple-element.346, f32[16,512]{1,0:T(8,128)S(1)} %get-tuple-element.301, f32[16,128]{1,0:T(8,128)S(1)} %get-tuple-element.302, ...), kind=kLoop, calls=%fused_computation.12.clone.1 | loop fusion | flops 27197440 | bytes 950336 | tf_op jit(solution)/shard_map/while/body/eval_jaxpr/reduce_sum | solution.py:36
  475.2 0.7 dynamic_slice.33
  476.9 18.4 %fusion.52 = f32[128,512]{1,0:T(8,128)S(1)} fusion(f32[128,512]{1,0:T(8,128)S(1)} %get-tuple-element.299, f32[128,512]{1,0:T(8,128)S(1)} %get-tuple-element.300, f32[16]{0:T(128)S(1)} %get-tuple-element.346, f32[16,512]{1,0:T(8,128)S(1)} %get-tuple-element.301, f32[16,128]{1,0:T(8,128)S(1)} %get-tuple-element.302, ...), kind=kLoop, calls=%fused_computation.12.clone.1 | loop fusion | flops 27197440 | bytes 950336 | tf_op jit(solution)/shard_map/while/body/eval_jaxpr/reduce_sum | solution.py:36
  495.5 0.7 dynamic_slice.33
  497.2 18.4 %fusion.52 = f32[128,512]{1,0:T(8,128)S(1)} fusion(f32[128,512]{1,0:T(8,128)S(1)} %get-tuple-element.299, f32[128,512]{1,0:T(8,128)S(1)} %get-tuple-element.300, f32[16]{0:T(128)S(1)} %get-tuple-element.346, f32[16,512]{1,0:T(8,128)S(1)} %get-tuple-element.301, f32[16,128]{1,0:T(8,128)S(1)} %get-tuple-element.302, ...), kind=kLoop, calls=%fused_computation.12.clone.1 | loop fusion | flops 27197440 | bytes 950336 | tf_op jit(solution)/shard_map/while/body/eval_jaxpr/reduce_sum | solution.py:36
  515.8 0.7 dynamic_slice.33
  517.5 18.4 %fusion.52 = f32[128,512]{1,0:T(8,128)S(1)} fusion(f32[128,512]{1,0:T(8,128)S(1)} %get-tuple-element.299, f32[128,512]{1,0:T(8,128)S(1)} %get-tuple-element.300, f32[16]{0:T(128)S(1)} %get-tuple-element.346, f32[16,512]{1,0:T(8,128)S(1)} %get-tuple-element.301, f32[16,128]{1,0:T(8,128)S(1)} %get-tuple-element.302, ...), kind=kLoop, calls=%fused_computation.12.clone.1 | loop fusion | flops 27197440 | bytes 950336 | tf_op jit(solution)/shard_map/while/body/eval_jaxpr/reduce_sum | solution.py:36
  536.1 0.7 dynamic_slice.33
  537.7 18.4 %fusion.52 = f32[128,512]{1,0:T(8,128)S(1)} fusion(f32[128,512]{1,0:T(8,128)S(1)} %get-tuple-element.299, f32[128,512]{1,0:T(8,128)S(1)} %get-tuple-element.300, f32[16]{0:T(128)S(1)} %get-tuple-element.346, f32[16,512]{1,0:T(8,128)S(1)} %get-tuple-element.301, f32[16,128]{1,0:T(8,128)S(1)} %get-tuple-element.302, ...), kind=kLoop, calls=%fused_computation.12.clone.1 | loop fusion | flops 27197440 | bytes 950336 | tf_op jit(solution)/shard_map/while/body/eval_jaxpr/reduce_sum | solution.py:36
  556.4 0.7 dynamic_slice.33
  558.0 18.4 %fusion.52 = f32[128,512]{1,0:T(8,128)S(1)} fusion(f32[128,512]{1,0:T(8,128)S(1)} %get-tuple-element.299, f32[128,512]{1,0:T(8,128)S(1)} %get-tuple-element.300, f32[16]{0:T(128)S(1)} %get-tuple-element.346, f32[16,512]{1,0:T(8,128)S(1)} %get-tuple-element.301, f32[16,128]{1,0:T(8,128)S(1)} %get-tuple-element.302, ...), kind=kLoop, calls=%fused_computation.12.clone.1 | loop fusion | flops 27197440 | bytes 950336 | tf_op jit(solution)/shard_map/while/body/eval_jaxpr/reduce_sum | solution.py:36
  576.9 12.1 %scatter_custom_fusion.1 = f32[3,512]{0,1:T(8,128)} fusion(s32[2048]{0:T(1024)S(1)} %bitcast.34, f32[2048,3]{1,0:T(8,128)S(1)} %bitcast.30, f32[]{:T(128)} %constant.96.clone.1), kind=kCustom, calls=%fused_computation.72 | custom fusion | flops 6144 | bytes 6148 | tf_op jit(solution)/shard_map/scatter-add | solution.py:148
  589.1 82.1 %reduce-scatter.2.cloned.1.call-done = f32[3,32]{0,1:T(8,128)} async-done(((f32[3,512]{0,1:T(8,128)}), f32[3,32]{0,1:T(8,128)}) %reduce-scatter.2.cloned.1.call-update) | async-done | bytes 400 | tf_op jit(solution)/shard_map/reduce_scatter | solution.py:150
  671.1 1.4 copy.167
  (113 shorter events, 5.2 us)
Async XLA Ops:
  7.2 377.6 %all-gather.4.cloned.1.call-start = ((), (), s32[]{:S(2)}) async-start(), calls=%async_computation.2 | async-start | bytes 5406720 | tf_op jit(solution)/shard_map/all_gather | solution.py:128
  8.4 101.3 %copy-start.1 = (s32[16384]{0:T(1024)}, s32[16384]{0:T(1024)S(1)}, u32[]{:S(2)}) copy-start(s32[16384]{0:T(1024)S(1)} %reshape.315) | copy-start | bytes 196612
  10.0 94.4 %copy-start.4 = (f32[32,32]{0,1:T(8,128)}, f32[32,32]{0,1:T(8,128)S(1)}, u32[]{:S(2)}) copy-start(f32[32,32]{0,1:T(8,128)S(1)} %copy.146) | copy-start | bytes 12292
  49.3 0.6 copy-start.3
  112.1 1.0 copy-start
  112.1 1.2 copy-start.2
  112.1 1.3 copy-start.9
  132.2 73.7 %copy-start.7 = (f32[32,256]{1,0:T(8,128)S(1)}, f32[32,256]{1,0:T(8,128)}, u32[]{:S(2)}) copy-start(f32[32,256]{1,0:T(8,128)} %param.15) | copy-start | bytes 98308
  218.0 94.6 %copy-start.8 = (s32[4,512]{1,0:T(4,128)S(1)}, s32[4,512]{1,0:T(4,128)}, u32[]{:S(2)}) copy-start(s32[4,512]{1,0:T(4,128)} %param.17) | copy-start | bytes 24580
  311.9 359.2 %reduce-scatter.2.cloned.1.call-start = ((), (), s32[]{:S(2)}) async-start(), calls=%async_computation.1 | async-start | bytes 278528 | tf_op jit(solution)/shard_map/reduce_scatter | solution.py:150
  387.6 2.5 copy-start.5
  390.0 24.4 %copy-start.6 = (f32[32,32]{1,0:T(8,128)}, f32[32,32]{1,0:T(8,128)S(1)}, u32[]{:S(2)}) copy-start(f32[32,32]{1,0:T(8,128)S(1)} %fusion.41) | copy-start | bytes 12292
Sparse Core Ops, SparseCore 0:
  312.1 72.6 all-gather.3
  589.2 81.9 reduce-scatter.1
